TPU v7x, 256 devices: a whole 4x4x8 slice. The times are simulated.
256 devices in a mesh: opair: 8 (over y, core), vpair: 32 (over z, x).
Axes of the slice: x: 4, y: 4, z: 8, core: 2. Of those that a mesh axis runs over, the one named last changes fastest.
Arguments:
- amplitudes: bfloat16 [1600, 24, 1000], P('vpair', 'opair'), may hold values from -6 to 6
- ladder_ints: bfloat16 [24, 1000, 32, 1000], P('opair', None, 'vpair'), may hold values from -0.0390625 to 0.0390625
- cycle_amps: bfloat16 [24, 100, 512], P('opair'), may hold values from -6 to 6
- cycle_ints: bfloat16 [24, 100, 100000], P('opair', None, 'vpair'), may hold values from -0.125 to 0.125
- occ_blocks: int32 [8], replicated, may hold values from 1 to 33, 100 in all
- virt_blocks: int32 [8], replicated, may hold values from 1 to 250, 1000 in all
- occ_start: int32 [1], replicated, may hold values from 0 to 84
- virt_start: int32 [1], replicated, may hold values from 0 to 968
- eps_occ: float32 [100], replicated, may hold values from -1 to -0.25
- eps_virt: float32 [1000], replicated, may hold values from 0.25 to 1.5
Outputs:
- update: float32 [16, 32, 100, 1000], P('opair', 'vpair')
All inputs are finite; a program needn't handle non-finite values.
Results may differ from a plain program's by a relative error of at most 0.0004.
Values may be sent and summed in bfloat16 or wider, within the bound.
No kernel may reach another device: no remote copies, remote signals or barrier semaphores. Data moves between devices by JAX's collectives and lax.ppermute only.
A program may use at most 128 MiB of HBM per device.

v0:
```python
import jax
import jax.numpy as jnp
from jax import lax
from jax.sharding import PartitionSpec as P

NO = 100
NV = 1000
I_DEV = 2
A_DEV = 1


def irrep_of(blocks, index):
    bounds = jnp.cumsum(blocks)[:-1]
    return jnp.sum((index[:, None] >= bounds[None, :]).astype(jnp.int32), axis=1)


def shards(
    amplitudes,
    ladder_ints,
    cycle_amps,
    cycle_ints,
    occ_blocks,
    virt_blocks,
    occ_start,
    virt_start,
    eps_occ,
    eps_virt,
):
    i_win = I_DEV * lax.axis_size("opair")
    a_win = A_DEV * lax.axis_size("vpair")
    slab_depth = ladder_ints.shape[0] * ladder_ints.shape[1]
    ladder_flat = ladder_ints.reshape(slab_depth, A_DEV * NV)
    piece = lax.all_gather(amplitudes, "vpair", axis=0, tiled=True)
    ladder = jnp.dot(
        piece.reshape(piece.shape[0], slab_depth), ladder_flat, preferred_element_type=jnp.float32
    )
    ladder = ladder.reshape(i_win, NO, A_DEV, NV).transpose(0, 2, 1, 3)
    cycle = lax.dot_general(
        cycle_amps, cycle_ints, (((0, 1), (0, 1)), ((), ())), preferred_element_type=jnp.float32
    )
    cycle = cycle.reshape(i_win, a_win, cycle_ints.shape[2])
    moved = lax.all_to_all(cycle, "vpair", split_axis=1, concat_axis=2, tiled=True)
    joined = ladder + moved.reshape(i_win, A_DEV, NO, NV)
    resid = lax.psum_scatter(joined, "opair", scatter_dimension=0, tiled=True)
    first_occ = occ_start[0] + lax.axis_index("opair") * I_DEV
    first_virt = virt_start[0] + lax.axis_index("vpair") * A_DEV
    glob_i = first_occ + jnp.arange(I_DEV, dtype=jnp.int32)
    glob_a = first_virt + jnp.arange(A_DEV, dtype=jnp.int32)
    sym_i = irrep_of(occ_blocks, glob_i)
    sym_a = irrep_of(virt_blocks, glob_a)
    sym_j = irrep_of(occ_blocks, jnp.arange(NO, dtype=jnp.int32))
    sym_b = irrep_of(virt_blocks, jnp.arange(NV, dtype=jnp.int32))
    total_sym = jnp.bitwise_xor(
        jnp.bitwise_xor(sym_i[:, None, None, None], sym_a[None, :, None, None]),
        jnp.bitwise_xor(sym_j[None, None, :, None], sym_b[None, None, None, :]),
    )
    e_i = lax.dynamic_slice_in_dim(eps_occ, first_occ, I_DEV)
    e_a = lax.dynamic_slice_in_dim(eps_virt, first_virt, A_DEV)
    denom = (
        e_i[:, None, None, None]
        - e_a[None, :, None, None]
        + eps_occ[None, None, :, None]
        - eps_virt[None, None, None, :]
    )
    return jnp.where(total_sym == 0, resid / denom, jnp.float32(0.0))


def solution(mesh):
    placed = (
        P("vpair", "opair", None),
        P("opair", None, "vpair", None),
        P("opair", None, None),
        P("opair", None, "vpair"),
        P(),
        P(),
        P(),
        P(),
        P(),
        P(),
    )
    return jax.shard_map(
        shards,
        mesh=mesh,
        in_specs=placed,
        out_specs=P("opair", "vpair", None, None),
        check_vma=False,
    )
```

profile of v0, /device:TPU:1, one launch (start us, length us, event | category | flops | bytes accessed | tf_op | source)
XLA Modules:
  0.0 344.3 jit_solution(18329957632520818298)
XLA Ops:
  6.5 0.0 copy-start
  6.5 0.0 all-gather.2.cloned.1.call-start
  6.5 2.1 copy.25
  8.7 0.0 all-gather.2.cloned.1.call-update
  8.7 0.0 reduce-scatter.2.cloned.1.call-start
  8.8 0.0 copy-done
  8.8 2.9 fusion.2
  11.7 3.8 %copy.29 = f32[16,32,3125]{2,0,1:T(8,128)S(1)} copy(f32[16,32,3125]{2,1,0:T(8,128)S(1)} %bitcast.23) | data formatting | bytes 12800000 | tf_op jit(solution)/shard_map/reshape | solution.py:41
  15.5 217.0 %all_to_all.4 = f32[16,32,3125]{2,0,1:T(8,128)S(1)} all-to-all(f32[16,32,3125]{2,0,1:T(8,128)S(1)} %copy.29), channel_id=1, replica_groups=mesh['opair'=8,'vpair'=32] {'vpair'}, dimensions={1} | all-to-all | bytes 12800000 | tf_op jit(solution)/shard_map/all_to_all | solution.py:42
  232.5 4.7 %copy.30 = f32[16,32,3125]{2,1,0:T(8,128)} copy(f32[16,32,3125]{2,0,1:T(8,128)S(1)} %all_to_all.4) | data formatting | bytes 12800000 | tf_op jit(solution)/shard_map/all_to_all | solution.py:42
  237.2 8.7 %reshape.160 = f32[16,100,1000]{2,1,0:T(8,128)} reshape(f32[16,32,3125]{2,1,0:T(8,128)} %copy.30) | data formatting | bytes 12800000 | tf_op jit(solution)/shard_map/reshape | solution.py:43
  245.9 3.0 all-gather.2.cloned.1.call-done
  248.9 21.3 %reshape.163 = bf16[16,100,3000]{2,1,0:T(8,128)(2,1)} reshape(bf16[1600,3,1000]{2,1,0:T(4,128)(2,1)} %all-gather.2.cloned.1.call-done) | data formatting | bytes 19200000 | tf_op jit(solution)/shard_map/dot_general | solution.py:34
  270.2 0.0 copy-start.1
  270.2 18.1 %add_bitcast_fusion = f32[16,1,100,1000]{3,2,0,1:T(8,128)} fusion(f32[16,100,1000]{2,1,0:T(8,128)} %reshape.160, bf16[16,100,3000]{2,1,0:T(8,128)(2,1)} %reshape.163, bf16[3000,1000,1]{1,0,2:T(8,128)(2,1)} %bitcast.24), kind=kOutput, calls=%fused_computation | convolution fusion | flops 9601599488 | bytes 28400000 | tf_op jit(solution)/shard_map/dot_general | solution.py:34
  288.3 0.0 copy-start.4
  288.3 0.0 copy-start.5
  288.3 0.0 copy-start.2
  288.3 0.0 copy-start.3
  288.3 0.0 reduce-scatter.2.cloned.1.call-update
  289.6 0.0 copy-done.4
  289.6 0.2 reduce-window.6
  289.8 0.0 copy-done.5
  289.8 0.2 reduce-window.9
  290.0 0.0 copy-done.2
  290.0 0.6 dynamic_slice.7
  290.6 0.0 copy-done.3
  290.6 0.7 dynamic-slice_subtract_fusion
  291.3 0.6 fusion.1
  292.0 0.1 convert_reduce_fusion.1
  292.1 0.1 convert_reduce_fusion
  292.1 0.2 fusion
  292.3 0.6 broadcast_xor_fusion.1
  293.0 0.1 broadcast_add_fusion
  293.1 0.1 broadcast_xor_fusion
  293.2 41.1 %reduce-scatter.2.cloned.1.call-done = f32[2,1,100,1000]{3,2,0,1:T(8,128)} async-done(((f32[16,1,100,1000]{3,2,0,1:T(8,128)}), f32[2,1,100,1000]{3,2,0,1:T(8,128)}) %reduce-scatter.2.cloned.1.call-update) | async-done | bytes 800016 | tf_op jit(solution)/shard_map/reduce_scatter | solution.py:44
  334.2 1.5 divide_select_fusion
  335.7 1.7 copy.31
  337.4 0.0 copy-done.1
  (2 shorter events, 0.0 us)
Async XLA Ops:
  6.5 2.2 copy-start
  6.5 242.4 %all-gather.2.cloned.1.call-start = ((), (), s32[]{:S(2)}) async-start(), calls=%async_computation.2 | async-start | bytes 13516800 | tf_op jit(solution)/shard_map/all_gather | solution.py:33
  8.7 325.5 %reduce-scatter.2.cloned.1.call-start = ((), (), s32[]{:S(2)}) async-start(), calls=%async_computation.3 | async-start | bytes 7667712 | tf_op jit(solution)/shard_map/reduce_scatter | solution.py:44
  270.2 67.2 %copy-start.1 = (bf16[3,100,3125]{2,1,0:T(8,128)(2,1)S(1)}, bf16[3,100,3125]{2,1,0:T(8,128)(2,1)}, u32[]{:S(2)}) copy-start(bf16[3,100,3125]{2,1,0:T(8,128)(2,1)} %param.13) | copy-start | bytes 5625004
  288.3 1.4 copy-start.4
  288.3 1.6 copy-start.5
  288.3 1.7 copy-start.2
  288.3 2.3 copy-start.3
Sparse Core Ops, SparseCore 0:
  9.9 238.9 all-gather.1
  288.4 45.7 reduce-scatter.1
where the time goes:
time: 345 us; the launch traced here: 344 us
  blocking collectives  217 us (63%)
  waiting for transfers between devices  44.1 us (13%)
  local copies, waits for them, and re-layouts  42.9 us (12%)
  matrix products  21 us (6%)
  between operations  14.8 us (4%)
  other arithmetic  4.34 us (1%)
    all_to_all x1, blocking collectives, shards(): lax.all_to_all(cycle, 'vpair', split_axis=1, concat_axis=2, tiled=True)  217 us
    reduce_scatter x1, waiting for transfers between devices, shards(): resid = lax.psum_scatter(joined, 'opair', scatter_dimension=0, tiled=True)  41.1 us
    dot_general x1, local copies, waits for them, and re-layouts, shards(): jnp.dot(piece.reshape(piece.shape[0], slab_depth), ladder_flat, preferred...  21.3 us
    dot_general x1, matrix products, shards(): jnp.dot(piece.reshape(piece.shape[0], slab_depth), ladder_flat, preferred...  18.1 us
    reshape x1, local copies, waits for them, and re-layouts, shards(): joined = ladder + moved.reshape(i_win, A_DEV, NO, NV)  8.74 us
  transfers between devices with their start and end apart: 2, of which 2 were waited for; matrix products, arithmetic and copies ran while one was open for 7% of the time, Pallas kernels for 0%

commit v1 on v0

--- a/solution.py
+++ b/solution.py
@@ -29,19 +29,24 @@
     i_win = I_DEV * lax.axis_size("opair")
     a_win = A_DEV * lax.axis_size("vpair")
     slab_depth = ladder_ints.shape[0] * ladder_ints.shape[1]
+    jb_dev = cycle_ints.shape[2]
+    cycle = lax.dot_general(
+        cycle_amps, cycle_ints, (((0, 1), (0, 1)), ((), ())), preferred_element_type=jnp.float32
+    )
+    cycle = cycle.reshape(i_win, a_win, jb_dev)
+    cycle = lax.psum_scatter(cycle, "opair", scatter_dimension=0, tiled=True)
+    cycle = lax.all_to_all(cycle, "vpair", split_axis=1, concat_axis=2, tiled=True)
     ladder_flat = ladder_ints.reshape(slab_depth, A_DEV * NV)
     piece = lax.all_gather(amplitudes, "vpair", axis=0, tiled=True)
     ladder = jnp.dot(
         piece.reshape(piece.shape[0], slab_depth), ladder_flat, preferred_element_type=jnp.float32
     )
-    ladder = ladder.reshape(i_win, NO, A_DEV, NV).transpose(0, 2, 1, 3)
-    cycle = lax.dot_general(
-        cycle_amps, cycle_ints, (((0, 1), (0, 1)), ((), ())), preferred_element_type=jnp.float32
+    ladder = ladder.reshape(i_win, NO, A_DEV * NV)
+    ladder, cycle = lax.optimization_barrier((ladder, cycle))
+    ladder = lax.psum_scatter(ladder, "opair", scatter_dimension=0, tiled=True)
+    resid = ladder.reshape(I_DEV, NO, A_DEV, NV).transpose(0, 2, 1, 3) + cycle.reshape(
+        I_DEV, A_DEV, NO, NV
     )
-    cycle = cycle.reshape(i_win, a_win, cycle_ints.shape[2])
-    moved = lax.all_to_all(cycle, "vpair", split_axis=1, concat_axis=2, tiled=True)
-    joined = ladder + moved.reshape(i_win, A_DEV, NO, NV)
-    resid = lax.psum_scatter(joined, "opair", scatter_dimension=0, tiled=True)
     first_occ = occ_start[0] + lax.axis_index("opair") * I_DEV
     first_virt = virt_start[0] + lax.axis_index("vpair") * A_DEV
     glob_i = first_occ + jnp.arange(I_DEV, dtype=jnp.int32)

time: 345 us -> 252 us (0.73)
  blocking collectives: 217 us -> 41.4 us
  waiting for transfers between devices: 44.1 us -> 134 us
  local copies, waits for them, and re-layouts: 42.9 us -> 32.2 us
    all_to_all x1, blocking collectives: 217 us -> 41.4 us  [shards(): lax.all_to_all(cycle, 'vpair', split_axis=1, concat_axis=2, tiled=True)]
    reduce_scatter x1 -> x2, waiting for transfers between devices: 41.1 us -> 87.5 us  [the longest x1 48.5 us: shards(): cycle = lax.psum_scatter(cycle, 'opair', scatter_dimension=0, tiled=True)]
    all_gather x1, waiting for transfers between devices: 2.99 us -> 46.5 us  [shards(): piece = lax.all_gather(amplitudes, 'vpair', axis=0, tiled=True)]
    reshape x2 -> x1, local copies, waits for them, and re-layouts: 12.5 us -> 2.2 us  [shards(): cycle.reshape(I_DEV, A_DEV, NO, NV)]
  transfers between devices with their start and end apart: 2 -> 3, of which waited for: 2 -> 3; matrix products, arithmetic and copies ran while one was open for 7% -> 3% of each run, Pallas kernels for 0% -> 0%
where the time goes in v1:
time: 252 us; the launch traced here: 251 us
  waiting for transfers between devices  134 us (53%)
  blocking collectives  41.4 us (16%)
  local copies, waits for them, and re-layouts  32.2 us (13%)
  matrix products  22.5 us (9%)
  between operations  16.3 us (6%)
  other arithmetic  4.38 us (2%)
    reduce_scatter x1, waiting for transfers between devices, shards(): cycle = lax.psum_scatter(cycle, 'opair', scatter_dimension=0, tiled=True)  48.5 us
    all_gather x1, waiting for transfers between devices, shards(): piece = lax.all_gather(amplitudes, 'vpair', axis=0, tiled=True)  46.5 us
    all_to_all x1, blocking collectives, shards(): lax.all_to_all(cycle, 'vpair', split_axis=1, concat_axis=2, tiled=True)  41.4 us
    reduce_scatter x1, waiting for transfers between devices, shards(): ladder = lax.psum_scatter(ladder, 'opair', scatter_dimension=0, tiled=True)  38.9 us
    dot_general x1, local copies, waits for them, and re-layouts, shards(): jnp.dot(piece.reshape(piece.shape[0], slab_depth), ladder_flat, preferred...  21.3 us
    dot_general x1, matrix products, shards(): jnp.dot(piece.reshape(piece.shape[0], slab_depth), ladder_flat, preferred...  16.9 us
    dot_general x1, matrix products, shards(): lax.dot_general(cycle_amps, cycle_ints, (((0, 1), (0, 1)), ((), ())), pre...  5.61 us
  transfers between devices with their start and end apart: 3, of which 3 were waited for; matrix products, arithmetic and copies ran while one was open for 3% of the time, Pallas kernels for 0%

profile of v1, /device:TPU:1, one launch (start us, length us, event | category | flops | bytes accessed | tf_op | source)
XLA Modules:
  0.0 251.0 jit_solution(16633642571301173802)
XLA Ops:
  7.4 0.0 copy-start
  7.4 0.0 copy-start.1
  7.4 0.0 reduce-scatter.3.cloned.1.call-start
  7.4 1.5 copy-done
  8.9 5.6 %fusion.3 = f32[512,3125,1]{1,0,2:T(8,128)} fusion(bf16[3,100,512]{2,1,0:T(8,128)(2,1)} %param.12, bf16[3,100,3125]{2,1,0:T(8,128)(2,1)S(1)} %copy-done), kind=kOutput, calls=%fused_computation.18 | convolution fusion | flops 960000000 | bytes 8582200 | tf_op jit(solution)/shard_map/dot_general | solution.py:33
  14.5 0.0 reduce-scatter.3.cloned.1.call-update
  14.6 0.0 all-gather.2.cloned.1.call-start
  14.6 0.0 copy-done.1
  14.6 1.0 copy.31
  15.6 0.0 all-gather.2.cloned.1.call-update
  15.7 0.0 reduce-scatter.5.cloned.1.call-start
  15.7 48.5 %reduce-scatter.3.cloned.1.call-done = f32[2,32,3125]{2,1,0:T(8,128)} async-done(((f32[16,32,3125]{2,1,0:T(8,128)}), f32[2,32,3125]{2,1,0:T(8,128)}) %reduce-scatter.3.cloned.1.call-update) | async-done | bytes 800016 | tf_op jit(solution)/shard_map/reduce_scatter | solution.py:37
  64.3 1.8 copy.35
  66.0 41.4 %all_to_all.12 = f32[2,32,3125]{2,0,1:T(2,128)S(1)} all-to-all(f32[2,32,3125]{2,0,1:T(2,128)S(1)} %copy.35), channel_id=1, replica_groups=mesh['opair'=8,'vpair'=32] {'vpair'}, dimensions={1} | all-to-all | bytes 1600000 | tf_op jit(solution)/shard_map/all_to_all | solution.py:38
  107.5 0.1 copy.36
  107.5 2.0 all_to_all.10
  109.5 46.5 %all-gather.2.cloned.1.call-done = bf16[1600,3,1000]{2,1,0:T(4,128)(2,1)} async-done(((bf16[50,3,1000]{2,1,0:T(4,128)(2,1)}), bf16[1600,3,1000]{2,1,0:T(4,128)(2,1)}) %all-gather.2.cloned.1.call-update) | async-done | bytes 9600016 | tf_op jit(solution)/shard_map/all_gather | solution.py:40
  156.0 21.3 %reshape.155 = bf16[16,100,3000]{2,1,0:T(8,128)(2,1)} reshape(bf16[1600,3,1000]{2,1,0:T(4,128)(2,1)} %all-gather.2.cloned.1.call-done) | data formatting | bytes 19200000 | tf_op jit(solution)/shard_map/dot_general | solution.py:41
  177.3 16.9 %fusion.2 = f32[16,100,1000]{2,1,0:T(8,128)} fusion(bf16[16,100,3000]{2,1,0:T(8,128)(2,1)} %reshape.155, bf16[3000,1000,1]{1,0,2:T(8,128)(2,1)} %bitcast.26), kind=kOutput, calls=%fused_computation.17 | convolution fusion | flops 9600000000 | bytes 22000000 | tf_op jit(solution)/shard_map/dot_general | solution.py:41
  194.2 0.0 copy-start.4
  194.2 0.0 copy-start.5
  194.2 0.0 copy-start.2
  194.2 0.0 copy-start.3
  194.3 0.0 reduce-scatter.5.cloned.1.call-update
  195.6 0.0 copy-done.4
  195.6 0.2 reduce-window.9
  195.8 0.0 copy-done.5
  195.8 0.2 reduce-window.6
  196.0 0.0 copy-done.2
  196.0 0.6 dynamic_slice.7
  196.6 0.0 copy-done.3
  196.6 0.7 dynamic-slice_subtract_fusion
  197.3 0.7 fusion.1
  198.0 0.1 convert_reduce_fusion
  198.1 0.1 convert_reduce_fusion.1
  198.2 0.2 fusion
  198.4 0.6 broadcast_xor_fusion.1
  199.0 0.1 broadcast_add_fusion
  199.1 0.1 broadcast_xor_fusion
  199.2 2.2 reshape.152
  201.4 38.9 %reduce-scatter.5.cloned.1.call-done = f32[2,100,1000]{2,1,0:T(8,128)} async-done(((f32[16,100,1000]{2,1,0:T(8,128)}), f32[2,100,1000]{2,1,0:T(8,128)}) %reduce-scatter.5.cloned.1.call-update) | async-done | bytes 800016 | tf_op jit(solution)/shard_map/reduce_scatter | solution.py:46
  240.3 1.5 select_bitcast_fusion
  241.8 1.7 copy.37
  (2 shorter events, 0.0 us)
Async XLA Ops:
  7.4 1.6 copy-start
  7.4 7.2 %copy-start.1 = (bf16[50,3,1000]{2,0,1:T(8,128)(2,1)S(1)}, bf16[50,3,1000]{2,0,1:T(8,128)(2,1)}, u32[]{:S(2)}) copy-start(bf16[50,3,1000]{2,0,1:T(8,128)(2,1)} %param.10) | copy-start | bytes 900004
  7.4 56.9 %reduce-scatter.3.cloned.1.call-start = ((), (), s32[]{:S(2)}) async-start(), calls=%async_computation.4 | async-start | bytes 7372800 | tf_op jit(solution)/shard_map/reduce_scatter | solution.py:37
  14.6 141.5 %all-gather.2.cloned.1.call-start = ((), (), s32[]{:S(2)}) async-start(), calls=%async_computation.3 | async-start | bytes 13516800 | tf_op jit(solution)/shard_map/all_gather | solution.py:40
  15.7 224.6 %reduce-scatter.5.cloned.1.call-start = ((), (), s32[]{:S(2)}) async-start(), calls=%async_computation.5 | async-start | bytes 7667712 | tf_op jit(solution)/shard_map/reduce_scatter | solution.py:46
  194.2 1.4 copy-start.4
  194.2 1.6 copy-start.5
  194.2 1.7 copy-start.2
  194.2 2.4 copy-start.3
Sparse Core Ops, SparseCore 0:
  14.7 49.5 reduce-scatter.2
  194.4 45.8 reduce-scatter.4
Sparse Core Ops, SparseCore 1:
  17.6 138.4 all-gather.1

commit v2 on v1

--- a/solution.py
+++ b/solution.py
@@ -7,6 +7,7 @@
 NV = 1000
 I_DEV = 2
 A_DEV = 1
+N_CHUNK = 2
 
 
 def irrep_of(blocks, index):
@@ -33,17 +34,36 @@
     cycle = lax.dot_general(
         cycle_amps, cycle_ints, (((0, 1), (0, 1)), ((), ())), preferred_element_type=jnp.float32
     )
-    cycle = cycle.reshape(i_win, a_win, jb_dev)
-    cycle = lax.psum_scatter(cycle, "opair", scatter_dimension=0, tiled=True)
-    cycle = lax.all_to_all(cycle, "vpair", split_axis=1, concat_axis=2, tiled=True)
-    ladder_flat = ladder_ints.reshape(slab_depth, A_DEV * NV)
-    piece = lax.all_gather(amplitudes, "vpair", axis=0, tiled=True)
-    ladder = jnp.dot(
-        piece.reshape(piece.shape[0], slab_depth), ladder_flat, preferred_element_type=jnp.float32
-    )
-    ladder = ladder.reshape(i_win, NO, A_DEV * NV)
-    ladder, cycle = lax.optimization_barrier((ladder, cycle))
-    ladder = lax.psum_scatter(ladder, "opair", scatter_dimension=0, tiled=True)
+    cycle_part = cycle.reshape(i_win, a_win, jb_dev)
+    c_dev = ladder_ints.shape[0]
+    v_slab = ladder_ints.reshape(c_dev, ladder_ints.shape[1], A_DEV * NV)
+    p_dev = amplitudes.shape[0]
+    p_chunk = p_dev // N_CHUNK
+    parts = []
+    prev = None
+    for s in range(N_CHUNK):
+        loc = amplitudes[s * p_chunk : (s + 1) * p_chunk].transpose(1, 0, 2)
+        if prev is None:
+            loc, cycle_part = lax.optimization_barrier((loc, cycle_part))
+            cycle = lax.psum_scatter(cycle_part, "opair", scatter_dimension=0, tiled=True)
+        elif s == 1:
+            loc, _, cycle = lax.optimization_barrier((loc, prev, cycle))
+        else:
+            loc, _ = lax.optimization_barrier((loc, prev))
+        piece = lax.all_gather(loc, "vpair", axis=1, tiled=True)
+        prev = piece
+        part = lax.dot_general(
+            piece, v_slab, (((0, 2), (0, 1)), ((), ())), preferred_element_type=jnp.float32
+        )
+        part = part.reshape(i_win, NO // N_CHUNK, A_DEV * NV)
+        if s == 1:
+            cycle = lax.all_to_all(cycle, "vpair", split_axis=1, concat_axis=2, tiled=True)
+            part, parts[-1], cycle = lax.optimization_barrier((part, parts[-1], cycle))
+        elif parts:
+            part, parts[-1] = lax.optimization_barrier((part, parts[-1]))
+        parts.append(lax.psum_scatter(part, "opair", scatter_dimension=0, tiled=True))
+    parts = [q.reshape(I_DEV, NO // p_dev, p_chunk, A_DEV * NV) for q in parts]
+    ladder = jnp.stack(parts, axis=2).reshape(I_DEV, NO, A_DEV * NV)
     resid = ladder.reshape(I_DEV, NO, A_DEV, NV).transpose(0, 2, 1, 3) + cycle.reshape(
         I_DEV, A_DEV, NO, NV
     )

time: 252 us -> 266 us (1.056)
  waiting for transfers between devices: 134 us -> 163 us
  local copies, waits for them, and re-layouts: 32.2 us -> 13.6 us
  matrix products: 22.5 us -> 32.3 us
  blocking collectives: 41.4 us -> 32.1 us
    all_gather x1 -> x2, waiting for transfers between devices: 46.5 us -> 137 us  [shards(): piece = lax.all_gather(loc, 'vpair', axis=1, tiled=True)]
    reduce_scatter x2 -> x3, waiting for transfers between devices: 87.5 us -> 25.3 us  [the longest x2 25.3 us: shards(): lax.psum_scatter(part, 'opair', scatter_dimension=0, tiled=True)]
    dot_general x1 -> x0, local copies, waits for them, and re-layouts: 21.3 us -> none  [shards(): jnp.dot(piece.reshape(piece.shape[0], slab_depth), ladder_flat, preferred...]
    dot_general x1 -> x2, matrix products: 16.9 us -> 26.7 us  [shards(): lax.dot_general(piece, v_slab, (((0, 2), (0, 1)), ((), ())), preferred_el...]
    all_to_all x1, blocking collectives: 41.4 us -> 32.1 us  [shards(): lax.all_to_all(cycle, 'vpair', split_axis=1, concat_axis=2, tiled=True)]
    optimization_barrier x0 -> x2, local copies, waits for them, and re-layouts: none -> 2.73 us  [the longest x1 2.09 us: shards(): part, parts[-1], cycle = lax.optimization_barrier((part, parts[-1], cycle))]
  transfers between devices with their start and end apart: 3 -> 5, of which waited for: 3 -> 3; matrix products, arithmetic and copies ran while one was open for 3% -> 14% of each run, Pallas kernels for 0% -> 0%
where the time goes in v2:
time: 266 us; the launch traced here: 263 us
  waiting for transfers between devices  163 us (61%)
  matrix products  32.3 us (12%)
  blocking collectives  32.1 us (12%)
  between operations  16.4 us (6%)
  local copies, waits for them, and re-layouts  13.6 us (5%)
  other arithmetic  5.5 us (2%)
    all_gather x2, waiting for transfers between devices, shards(): piece = lax.all_gather(loc, 'vpair', axis=1, tiled=True)  137 us
    all_to_all x1, blocking collectives, shards(): lax.all_to_all(cycle, 'vpair', split_axis=1, concat_axis=2, tiled=True)  32.1 us
    dot_general x2, matrix products, shards(): lax.dot_general(piece, v_slab, (((0, 2), (0, 1)), ((), ())), preferred_el...  26.7 us
    reduce_scatter x2, waiting for transfers between devices, shards(): lax.psum_scatter(part, 'opair', scatter_dimension=0, tiled=True)  25.3 us
    dot_general x1, matrix products, shards(): lax.dot_general(cycle_amps, cycle_ints, (((0, 1), (0, 1)), ((), ())), pre...  5.67 us
  transfers between devices with their start and end apart: 5, of which 3 were waited for; matrix products, arithmetic and copies ran while one was open for 14% of the time, Pallas kernels for 0%

profile of v2, /device:TPU:1, one launch (start us, length us, event | category | flops | bytes accessed | tf_op | source)
XLA Modules:
  0.0 263.5 jit_solution(7617233664805227034)
XLA Ops:
  7.4 0.0 copy-start
  7.4 0.0 all-gather.3.cloned.1.call-start
  7.4 1.2 fusion.19
  8.6 0.8 copy.72
  9.4 0.0 copy-done
  9.4 5.7 %fusion.20 = f32[512,3125,1]{1,0,2:T(8,128)} fusion(bf16[3,100,512]{2,1,0:T(8,128)(2,1)} %param.12, bf16[3,100,3125]{2,1,0:T(8,128)(2,1)S(1)} %copy-done), kind=kOutput, calls=%fused_computation.30 | convolution fusion | flops 960000000 | bytes 8582200 | tf_op jit(solution)/shard_map/dot_general | solution.py:34
  15.1 0.0 all-gather.3.cloned.1.call-update
  15.1 0.0 reduce-scatter.4.cloned.1.call-start
  15.2 0.5 reduce-scatter.4.cloned.1.call-update
  15.7 0.0 all-gather.5.cloned.1.call-start
  15.7 0.8 copy.73
  16.6 91.4 %all-gather.3.cloned.1.call-done = bf16[3,800,1000]{2,0,1:T(4,128)(2,1)} async-done(((bf16[3,25,1000]{2,0,1:T(4,128)(2,1)}), bf16[3,800,1000]{2,0,1:T(4,128)(2,1)}) %all-gather.3.cloned.1.call-update) | async-done | bytes 4800016 | tf_op jit(solution)/shard_map/all_gather | solution.py:53
  108.0 0.0 reduce-scatter.4.cloned.1.call-done
  108.0 0.0 all-gather.5.cloned.1.call-update
  108.0 0.0 reduce-scatter.6.cloned.1.call-start
  108.1 0.0 copy-start.1
  108.1 13.3 %fusion.11 = f32[16,50,1000]{2,1,0:T(8,128)} fusion(bf16[3,1000,1,1000]{3,1,2,0:T(8,128)(2,1)} %param.11, bf16[16,50,3,1000]{3,2,1,0:T(4,128)(2,1)} %bitcast.55), kind=kOutput, calls=%fused_computation.7 | convolution fusion | flops 4800000000 | bytes 14000000 | tf_op jit(solution)/shard_map/dot_general | solution.py:55
  121.4 0.0 reduce-scatter.6.cloned.1.call-update
  121.4 0.0 reduce-scatter.8.cloned.1.call-start
  121.5 0.0 copy-done.1
  121.5 0.6 copy.43
  122.1 32.1 %all_to_all.12 = f32[2,32,3125]{2,0,1:T(2,128)S(1)} all-to-all(f32[2,32,3125]{2,0,1:T(2,128)S(1)} %copy.43), channel_id=1, replica_groups=mesh['opair'=8,'vpair'=32] {'vpair'}, dimensions={1} | all-to-all | bytes 1600000 | tf_op jit(solution)/shard_map/all_to_all | solution.py:60
  154.3 0.1 copy.44
  154.3 2.0 all_to_all.10
  156.3 46.0 %all-gather.5.cloned.1.call-done = bf16[3,800,1000]{2,0,1:T(4,128)(2,1)} async-done(((bf16[3,25,1000]{2,0,1:T(4,128)(2,1)}), bf16[3,800,1000]{2,0,1:T(4,128)(2,1)}) %all-gather.5.cloned.1.call-update) | async-done | bytes 4800016 | tf_op jit(solution)/shard_map/all_gather | solution.py:53
  202.3 0.0 copy-start.4
  202.3 0.0 copy-start.5
  202.3 0.0 copy-start.2
  202.3 0.0 copy-start.3
  202.3 13.3 %fusion.6 = f32[16,50,1000]{2,1,0:T(8,128)} fusion(bf16[3,1000,1,1000]{3,1,2,0:T(8,128)(2,1)} %param.11, bf16[16,50,3,1000]{3,2,1,0:T(4,128)(2,1)} %bitcast.56), kind=kOutput, calls=%fused_computation.6 | convolution fusion | flops 4800000000 | bytes 14000000 | tf_op jit(solution)/shard_map/dot_general | solution.py:55
  215.6 0.0 reduce-scatter.6.cloned.1.call-done
  215.6 0.0 reduce-scatter.8.cloned.1.call-update
  216.9 0.0 copy-done.4
  217.0 0.2 reduce-window.6
  217.1 0.0 copy-done.5
  217.1 0.2 reduce-window.9
  217.3 0.0 copy-done.2
  217.3 0.6 dynamic_slice.7
  218.0 0.0 copy-done.3
  218.0 0.7 dynamic-slice_subtract_fusion
  218.7 0.7 fusion.18
  219.4 0.1 convert_reduce_fusion
  219.5 0.1 convert_reduce_fusion.1
  219.6 0.2 fusion.17
  219.8 0.7 broadcast_xor_fusion.1
  220.5 0.1 broadcast_add_fusion
  220.6 0.1 broadcast_xor_fusion
  220.7 2.1 copy.45
  222.7 2.2 reshape.185
  224.9 25.3 %reduce-scatter.8.cloned.1.call-done = f32[2,50,1000]{2,1,0:T(8,128)} async-done(((f32[16,50,1000]{2,1,0:T(8,128)}), f32[2,50,1000]{2,1,0:T(8,128)}) %reduce-scatter.8.cloned.1.call-update) | async-done | bytes 400016 | tf_op jit(solution)/shard_map/reduce_scatter | solution.py:64
  250.2 1.3 copy.46
  251.6 1.4 pad_maximum_fusion
  253.0 0.1 copy.47
  253.0 1.1 compare_select_fusion
  254.2 1.7 copy.49
  (2 shorter events, 0.0 us)
Async XLA Ops:
  7.4 2.0 copy-start
  7.4 100.6 %all-gather.3.cloned.1.call-start = ((), (), s32[]{:S(2)}) async-start(), calls=%async_computation.4 | async-start | bytes 6758400 | tf_op jit(solution)/shard_map/all_gather | solution.py:53
  15.1 92.9 %reduce-scatter.4.cloned.1.call-start = ((), (), s32[]{:S(2)}) async-start(), calls=%async_computation.5 | async-start | bytes 7372800 | tf_op jit(solution)/shard_map/reduce_scatter | solution.py:48
  15.7 186.6 %all-gather.5.cloned.1.call-start = ((), (), s32[]{:S(2)}) async-start(), calls=%async_computation.6 | async-start | bytes 6758400 | tf_op jit(solution)/shard_map/all_gather | solution.py:53
  108.0 107.6 %reduce-scatter.6.cloned.1.call-start = ((), (), s32[]{:S(2)}) async-start(), calls=%async_computation.7 | async-start | bytes 4128768 | tf_op jit(solution)/shard_map/reduce_scatter | solution.py:64
  108.1 13.4 %copy-start.1 = (f32[2,32,3125]{2,1,0:T(8,128)S(1)}, f32[2,32,3125]{2,1,0:T(8,128)}, u32[]{:S(2)}) copy-start(f32[2,32,3125]{2,1,0:T(8,128)} %reduce-scatter.4.cloned.1.call-done) | copy-start | bytes 2400004
  121.4 128.8 %reduce-scatter.8.cloned.1.call-start = ((), (), s32[]{:S(2)}) async-start(), calls=%async_computation.8 | async-start | bytes 4128768 | tf_op jit(solution)/shard_map/reduce_scatter | solution.py:64
  202.3 14.7 %copy-start.4 = (s32[8]{0:T(128)S(1)}, s32[8]{0:T(128)}, u32[]{:S(2)}) copy-start(s32[8]{0:T(128)} %param.14) | copy-start | bytes 100
  202.3 14.9 %copy-start.5 = (s32[8]{0:T(128)S(1)}, s32[8]{0:T(128)}, u32[]{:S(2)}) copy-start(s32[8]{0:T(128)} %param.15) | copy-start | bytes 100
  202.3 15.1 %copy-start.2 = (f32[1000]{0:T(1024)S(1)}, f32[1000]{0:T(1024)}, u32[]{:S(2)}) copy-start(f32[1000]{0:T(1024)} %param.19) | copy-start | bytes 12004
  202.3 15.7 %copy-start.3 = (f32[100]{0:T(128)S(1)}, f32[100]{0:T(128)}, u32[]{:S(2)}) copy-start(f32[100]{0:T(128)} %param.18) | copy-start | bytes 1204
Sparse Core Ops, SparseCore 0:
  15.2 92.7 all-gather.2
  110.6 91.6 all-gather.4
Sparse Core Ops, SparseCore 1:
  18.2 49.5 reduce-scatter.3
  121.5 35.2 reduce-scatter.5
  215.7 34.5 reduce-scatter.7

commit v3 on v1

--- a/solution.py
+++ b/solution.py
@@ -33,13 +33,14 @@
     cycle = lax.dot_general(
         cycle_amps, cycle_ints, (((0, 1), (0, 1)), ((), ())), preferred_element_type=jnp.float32
     )
-    cycle = cycle.reshape(i_win, a_win, jb_dev)
-    cycle = lax.psum_scatter(cycle, "opair", scatter_dimension=0, tiled=True)
+    cycle_part = cycle.reshape(i_win, a_win, jb_dev)
+    cycle = lax.psum_scatter(cycle_part, "opair", scatter_dimension=0, tiled=True)
     cycle = lax.all_to_all(cycle, "vpair", split_axis=1, concat_axis=2, tiled=True)
-    ladder_flat = ladder_ints.reshape(slab_depth, A_DEV * NV)
+    c_dev = ladder_ints.shape[0]
+    v_slab = ladder_ints.reshape(c_dev, ladder_ints.shape[1], A_DEV * NV)
     piece = lax.all_gather(amplitudes, "vpair", axis=0, tiled=True)
-    ladder = jnp.dot(
-        piece.reshape(piece.shape[0], slab_depth), ladder_flat, preferred_element_type=jnp.float32
+    ladder = lax.dot_general(
+        piece, v_slab, (((1, 2), (0, 1)), ((), ())), preferred_element_type=jnp.float32
     )
     ladder = ladder.reshape(i_win, NO, A_DEV * NV)
     ladder, cycle = lax.optimization_barrier((ladder, cycle))

time: 252 us -> 236 us (0.937)
  local copies, waits for them, and re-layouts: 32.2 us -> 10.9 us
  matrix products: 22.5 us -> 28.4 us
    dot_general x1 -> x0, local copies, waits for them, and re-layouts: 21.3 us -> none  [shards(): jnp.dot(piece.reshape(piece.shape[0], slab_depth), ladder_flat, preferred...]
    dot_general x1, matrix products: 16.9 us -> 22.8 us  [shards(): lax.dot_general(piece, v_slab, (((1, 2), (0, 1)), ((), ())), preferred_el...]
  transfers between devices with their start and end apart: 3 -> 3, of which waited for: 3 -> 3; matrix products, arithmetic and copies ran while one was open for 3% -> 4% of each run, Pallas kernels for 0% -> 0%
where the time goes in v3:
time: 236 us
  waiting for transfers between devices  134 us (57%)
  blocking collectives  41.4 us (18%)
  matrix products  28.4 us (12%)
  between operations  16.3 us (7%)
  local copies, waits for them, and re-layouts  10.9 us (5%)
  other arithmetic  4.38 us (2%)
    reduce_scatter x1, waiting for transfers between devices, shards(): lax.psum_scatter(cycle_part, 'opair', scatter_dimension=0, tiled=True)  48.5 us
    all_gather x1, waiting for transfers between devices, shards(): piece = lax.all_gather(amplitudes, 'vpair', axis=0, tiled=True)  46.5 us
    all_to_all x1, blocking collectives, shards(): lax.all_to_all(cycle, 'vpair', split_axis=1, concat_axis=2, tiled=True)  41.4 us
    reduce_scatter x1, waiting for transfers between devices, shards(): ladder = lax.psum_scatter(ladder, 'opair', scatter_dimension=0, tiled=True)  38.9 us
    dot_general x1, matrix products, shards(): lax.dot_general(piece, v_slab, (((1, 2), (0, 1)), ((), ())), preferred_el...  22.8 us
    dot_general x1, matrix products, shards(): lax.dot_general(cycle_amps, cycle_ints, (((0, 1), (0, 1)), ((), ())), pre...  5.61 us
  transfers between devices with their start and end apart: 3, of which 3 were waited for; matrix products, arithmetic and copies ran while one was open for 4% of the time, Pallas kernels for 0%

profile of v3, /device:TPU:1, one launch (start us, length us, event | category | flops | bytes accessed | tf_op | source)
XLA Modules:
  0.0 235.5 jit_solution(17980781202638052548)
XLA Ops:
  7.4 0.0 copy-start
  7.4 0.0 copy-start.1
  7.4 0.0 reduce-scatter.3.cloned.1.call-start
  7.4 1.5 copy-done
  8.9 5.6 %fusion.10 = f32[512,3125,1]{1,0,2:T(8,128)} fusion(bf16[3,100,512]{2,1,0:T(8,128)(2,1)} %param.12, bf16[3,100,3125]{2,1,0:T(8,128)(2,1)S(1)} %copy-done), kind=kOutput, calls=%fused_computation.21 | convolution fusion | flops 960000000 | bytes 8582200 | tf_op jit(solution)/shard_map/dot_general | solution.py:33
  14.5 0.0 reduce-scatter.3.cloned.1.call-update
  14.6 0.0 all-gather.2.cloned.1.call-start
  14.6 0.0 copy-done.1
  14.6 1.0 copy.27
  15.6 0.0 all-gather.2.cloned.1.call-update
  15.7 0.0 reduce-scatter.5.cloned.1.call-start
  15.7 48.5 %reduce-scatter.3.cloned.1.call-done = f32[2,32,3125]{2,1,0:T(8,128)} async-done(((f32[16,32,3125]{2,1,0:T(8,128)}), f32[2,32,3125]{2,1,0:T(8,128)}) %reduce-scatter.3.cloned.1.call-update) | async-done | bytes 800016 | tf_op jit(solution)/shard_map/reduce_scatter | solution.py:37
  64.3 1.8 copy.30
  66.0 41.4 %all_to_all.12 = f32[2,32,3125]{2,0,1:T(2,128)S(1)} all-to-all(f32[2,32,3125]{2,0,1:T(2,128)S(1)} %copy.30), channel_id=1, replica_groups=mesh['opair'=8,'vpair'=32] {'vpair'}, dimensions={1} | all-to-all | bytes 1600000 | tf_op jit(solution)/shard_map/all_to_all | solution.py:38
  107.5 0.1 copy.31
  107.5 2.0 all_to_all.10
  109.5 46.5 %all-gather.2.cloned.1.call-done = bf16[1600,3,1000]{2,1,0:T(4,128)(2,1)} async-done(((bf16[50,3,1000]{2,1,0:T(4,128)(2,1)}), bf16[1600,3,1000]{2,1,0:T(4,128)(2,1)}) %all-gather.2.cloned.1.call-update) | async-done | bytes 9600016 | tf_op jit(solution)/shard_map/all_gather | solution.py:41
  156.0 22.8 %fusion.3 = f32[16,100,1000]{2,1,0:T(8,128)} fusion(bf16[3,1000,1,1000]{3,1,2,0:T(8,128)(2,1)} %param.11, bf16[16,100,3,1000]{3,2,1,0:T(4,128)(2,1)} %bitcast.32), kind=kOutput, calls=%fused_computation.3 | convolution fusion | flops 9600000000 | bytes 22000000 | tf_op jit(solution)/shard_map/dot_general | solution.py:42
  178.8 0.0 copy-start.4
  178.8 0.0 copy-start.5
  178.8 0.0 copy-start.2
  178.8 0.0 copy-start.3
  178.8 0.0 reduce-scatter.5.cloned.1.call-update
  180.2 0.0 copy-done.4
  180.2 0.2 reduce-window.9
  180.4 0.0 copy-done.5
  180.4 0.2 reduce-window.6
  180.5 0.0 copy-done.2
  180.5 0.6 dynamic_slice.7
  181.2 0.0 copy-done.3
  181.2 0.7 dynamic-slice_subtract_fusion
  181.9 0.7 fusion.9
  182.5 0.1 convert_reduce_fusion
  182.6 0.1 convert_reduce_fusion.1
  182.7 0.2 fusion.8
  182.9 0.6 broadcast_xor_fusion.1
  183.5 0.1 broadcast_add_fusion
  183.6 0.1 broadcast_xor_fusion
  183.7 2.2 reshape.150
  185.9 38.9 %reduce-scatter.5.cloned.1.call-done = f32[2,100,1000]{2,1,0:T(8,128)} async-done(((f32[16,100,1000]{2,1,0:T(8,128)}), f32[2,100,1000]{2,1,0:T(8,128)}) %reduce-scatter.5.cloned.1.call-update) | async-done | bytes 800016 | tf_op jit(solution)/shard_map/reduce_scatter | solution.py:47
  224.9 1.5 select_bitcast_fusion
  226.4 1.7 copy.32
  (2 shorter events, 0.0 us)
Async XLA Ops:
  7.4 1.6 copy-start
  7.4 7.2 %copy-start.1 = (bf16[50,3,1000]{2,0,1:T(8,128)(2,1)S(1)}, bf16[50,3,1000]{2,0,1:T(8,128)(2,1)}, u32[]{:S(2)}) copy-start(bf16[50,3,1000]{2,0,1:T(8,128)(2,1)} %param.10) | copy-start | bytes 900004
  7.4 56.9 %reduce-scatter.3.cloned.1.call-start = ((), (), s32[]{:S(2)}) async-start(), calls=%async_computation.4 | async-start | bytes 7372800 | tf_op jit(solution)/shard_map/reduce_scatter | solution.py:37
  14.6 141.5 %all-gather.2.cloned.1.call-start = ((), (), s32[]{:S(2)}) async-start(), calls=%async_computation.3 | async-start | bytes 13516800 | tf_op jit(solution)/shard_map/all_gather | solution.py:41
  15.7 209.2 %reduce-scatter.5.cloned.1.call-start = ((), (), s32[]{:S(2)}) async-start(), calls=%async_computation.5 | async-start | bytes 7667712 | tf_op jit(solution)/shard_map/reduce_scatter | solution.py:47
  178.8 1.4 copy-start.4
  178.8 1.6 copy-start.5
  178.8 1.7 copy-start.2
  178.8 2.4 copy-start.3
Sparse Core Ops, SparseCore 0:
  14.7 49.5 reduce-scatter.2
  179.0 45.8 reduce-scatter.4
Sparse Core Ops, SparseCore 1:
  17.6 138.4 all-gather.1

commit v4 on v3

--- a/solution.py
+++ b/solution.py
@@ -30,18 +30,19 @@
     a_win = A_DEV * lax.axis_size("vpair")
     slab_depth = ladder_ints.shape[0] * ladder_ints.shape[1]
     jb_dev = cycle_ints.shape[2]
+    amps_rows = amplitudes.reshape(amplitudes.shape[0], slab_depth)
+    amps_rows, cycle_amps = lax.optimization_barrier((amps_rows, cycle_amps))
     cycle = lax.dot_general(
         cycle_amps, cycle_ints, (((0, 1), (0, 1)), ((), ())), preferred_element_type=jnp.float32
     )
     cycle_part = cycle.reshape(i_win, a_win, jb_dev)
     cycle = lax.psum_scatter(cycle_part, "opair", scatter_dimension=0, tiled=True)
     cycle = lax.all_to_all(cycle, "vpair", split_axis=1, concat_axis=2, tiled=True)
-    c_dev = ladder_ints.shape[0]
-    v_slab = ladder_ints.reshape(c_dev, ladder_ints.shape[1], A_DEV * NV)
-    piece = lax.all_gather(amplitudes, "vpair", axis=0, tiled=True)
-    ladder = lax.dot_general(
-        piece, v_slab, (((1, 2), (0, 1)), ((), ())), preferred_element_type=jnp.float32
+    v_flat = ladder_ints.reshape(slab_depth, A_DEV * NV)
+    piece = lax.all_gather(
+        amps_rows, "vpair", axis=0, tiled=True
     )
+    ladder = jnp.dot(piece, v_flat, preferred_element_type=jnp.float32)
     ladder = ladder.reshape(i_win, NO, A_DEV * NV)
     ladder, cycle = lax.optimization_barrier((ladder, cycle))
     ladder = lax.psum_scatter(ladder, "opair", scatter_dimension=0, tiled=True)
@@ -84,6 +85,7 @@
         P(),
         P(),
     )
+
     return jax.shard_map(
         shards,
         mesh=mesh,

time: 236 us -> 236 us (level)
  local copies, waits for them, and re-layouts: 10.9 us -> 25.4 us
  waiting for transfers between devices: 134 us -> 125 us
  matrix products: 28.4 us -> 22.6 us
    dot_general x0 -> x1, local copies, waits for them, and re-layouts: none -> 14.4 us  [shards(): ladder = jnp.dot(piece, v_flat, preferred_element_type=jnp.float32)]
    all_gather x1, waiting for transfers between devices: 46.5 us -> 36.6 us  [shards(): piece = lax.all_gather(amps_rows, 'vpair', axis=0, tiled=True)]
    dot_general x1, matrix products: 22.8 us -> 16.9 us  [shards(): ladder = jnp.dot(piece, v_flat, preferred_element_type=jnp.float32)]
  transfers between devices with their start and end apart: 3 -> 3, of which waited for: 3 -> 3; matrix products, arithmetic and copies ran while one was open for 4% -> 3% of each run, Pallas kernels for 0% -> 0%
where the time goes in v4:
time: 236 us; the launch traced here: 235 us
  waiting for transfers between devices  125 us (53%)
  blocking collectives  41.5 us (18%)
  local copies, waits for them, and re-layouts  25.4 us (11%)
  matrix products  22.6 us (10%)
  between operations  16.3 us (7%)
  other arithmetic  4.38 us (2%)
    reduce_scatter x1, waiting for transfers between devices, shards(): lax.psum_scatter(cycle_part, 'opair', scatter_dimension=0, tiled=True)  49.1 us
    all_to_all x1, blocking collectives, shards(): lax.all_to_all(cycle, 'vpair', split_axis=1, concat_axis=2, tiled=True)  41.5 us
    reduce_scatter x1, waiting for transfers between devices, shards(): ladder = lax.psum_scatter(ladder, 'opair', scatter_dimension=0, tiled=True)  38.9 us
    all_gather x1, waiting for transfers between devices, shards(): piece = lax.all_gather(amps_rows, 'vpair', axis=0, tiled=True)  36.6 us
    dot_general x1, matrix products, shards(): ladder = jnp.dot(piece, v_flat, preferred_element_type=jnp.float32)  16.9 us
    dot_general x1, local copies, waits for them, and re-layouts, shards(): ladder = jnp.dot(piece, v_flat, preferred_element_type=jnp.float32)  14.4 us
    dot_general x1, matrix products, shards(): lax.dot_general(cycle_amps, cycle_ints, (((0, 1), (0, 1)), ((), ())), pre...  5.64 us
  transfers between devices with their start and end apart: 3, of which 3 were waited for; matrix products, arithmetic and copies ran while one was open for 3% of the time, Pallas kernels for 0%

profile of v4, /device:TPU:1, one launch (start us, length us, event | category | flops | bytes accessed | tf_op | source)
XLA Modules:
  0.0 235.2 jit_solution(9388965948902432185)
XLA Ops:
  7.4 0.0 copy-start
  7.4 0.0 reduce-scatter.3.cloned.1.call-start
  7.4 1.4 copy.25
  8.8 1.2 reshape.151
  10.0 0.0 copy-done
  10.0 5.6 %fusion.3 = f32[512,3125,1]{1,0,2:T(8,128)} fusion(bf16[3,100,512]{2,1,0:T(8,128)(2,1)} %param.12, bf16[3,100,3125]{2,1,0:T(8,128)(2,1)S(1)} %copy-done), kind=kOutput, calls=%fused_computation.18 | convolution fusion | flops 960000000 | bytes 8582200 | tf_op jit(solution)/shard_map/dot_general | solution.py:35
  15.6 0.0 reduce-scatter.3.cloned.1.call-update
  15.7 0.0 all-gather.3.cloned.1.call-start
  15.7 0.5 all-gather.3.cloned.1.call-update
  16.3 0.0 reduce-scatter.5.cloned.1.call-start
  16.3 49.1 %reduce-scatter.3.cloned.1.call-done = f32[2,32,3125]{2,1,0:T(8,128)} async-done(((f32[16,32,3125]{2,1,0:T(8,128)}), f32[2,32,3125]{2,1,0:T(8,128)}) %reduce-scatter.3.cloned.1.call-update) | async-done | bytes 800016 | tf_op jit(solution)/shard_map/reduce_scatter | solution.py:39
  65.4 1.8 copy.27
  67.2 41.5 %all_to_all.12 = f32[2,32,3125]{2,0,1:T(2,128)S(1)} all-to-all(f32[2,32,3125]{2,0,1:T(2,128)S(1)} %copy.27), channel_id=1, replica_groups=mesh['opair'=8,'vpair'=32] {'vpair'}, dimensions={1} | all-to-all | bytes 1600000 | tf_op jit(solution)/shard_map/all_to_all | solution.py:40
  108.6 0.1 copy.28
  108.7 2.0 all_to_all.10
  110.6 36.6 %all-gather.3.cloned.1.call-done = bf16[32,50,3000]{2,1,0:T(8,128)(2,1)} async-done(((bf16[1,50,3000]{2,1,0:T(8,128)(2,1)}), bf16[32,50,3000]{2,1,0:T(8,128)(2,1)}) %all-gather.3.cloned.1.call-update) | async-done | bytes 9600016 | tf_op jit(solution)/shard_map/all_gather | solution.py:42
  147.2 14.4 %dot_general.8 = bf16[16,100,3000]{2,1,0:T(8,128)(2,1)} reshape(bf16[32,50,3000]{2,1,0:T(8,128)(2,1)} %all-gather.3.cloned.1.call-done) | data formatting | bytes 19200000 | tf_op jit(solution)/shard_map/dot_general | solution.py:45
  161.6 16.9 %fusion.2 = f32[16,100,1000]{2,1,0:T(8,128)} fusion(bf16[16,100,3000]{2,1,0:T(8,128)(2,1)} %dot_general.8, bf16[3000,1000,1]{1,0,2:T(8,128)(2,1)} %bitcast.28), kind=kOutput, calls=%fused_computation.17 | convolution fusion | flops 9600000000 | bytes 22000000 | tf_op jit(solution)/shard_map/dot_general | solution.py:45
  178.5 0.0 copy-start.3
  178.5 0.0 copy-start.4
  178.5 0.0 copy-start.1
  178.5 0.0 copy-start.2
  178.5 0.0 reduce-scatter.5.cloned.1.call-update
  179.9 0.0 copy-done.3
  179.9 0.2 reduce-window.9
  180.1 0.0 copy-done.4
  180.1 0.2 reduce-window.6
  180.3 0.0 copy-done.1
  180.3 0.6 dynamic_slice.7
  180.9 0.0 copy-done.2
  180.9 0.7 dynamic-slice_subtract_fusion
  181.6 0.7 fusion.1
  182.3 0.1 convert_reduce_fusion
  182.4 0.1 convert_reduce_fusion.1
  182.5 0.2 fusion
  182.6 0.6 broadcast_xor_fusion.1
  183.3 0.1 broadcast_add_fusion
  183.3 0.1 broadcast_xor_fusion
  183.4 2.2 reshape.154
  185.7 38.9 %reduce-scatter.5.cloned.1.call-done = f32[2,100,1000]{2,1,0:T(8,128)} async-done(((f32[16,100,1000]{2,1,0:T(8,128)}), f32[2,100,1000]{2,1,0:T(8,128)}) %reduce-scatter.5.cloned.1.call-update) | async-done | bytes 800016 | tf_op jit(solution)/shard_map/reduce_scatter | solution.py:48
  224.6 1.5 select_bitcast_fusion
  226.1 1.7 copy.29
  (2 shorter events, 0.0 us)
Async XLA Ops:
  7.4 2.6 %copy-start = (bf16[3,100,3125]{2,1,0:T(8,128)(2,1)S(1)}, bf16[3,100,3125]{2,1,0:T(8,128)(2,1)}, u32[]{:S(2)}) copy-start(bf16[3,100,3125]{2,1,0:T(8,128)(2,1)} %param.13) | copy-start | bytes 5625004
  7.4 58.0 %reduce-scatter.3.cloned.1.call-start = ((), (), s32[]{:S(2)}) async-start(), calls=%async_computation.3 | async-start | bytes 7372800 | tf_op jit(solution)/shard_map/reduce_scatter | solution.py:39
  15.7 131.5 %all-gather.3.cloned.1.call-start = ((), (), s32[]{:S(2)}) async-start(), calls=%async_computation.5 | async-start | bytes 11354112 | tf_op jit(solution)/shard_map/all_gather | solution.py:42
  16.3 208.3 %reduce-scatter.5.cloned.1.call-start = ((), (), s32[]{:S(2)}) async-start(), calls=%async_computation.4 | async-start | bytes 7667712 | tf_op jit(solution)/shard_map/reduce_scatter | solution.py:48
  178.5 1.4 copy-start.3
  178.5 1.6 copy-start.4
  178.5 1.7 copy-start.1
  178.5 2.4 %copy-start.2 = (f32[100]{0:T(128)S(1)}, f32[100]{0:T(128)}, u32[]{:S(2)}) copy-start(f32[100]{0:T(128)} %param.18) | copy-start | bytes 1204
Sparse Core Ops, SparseCore 0:
  15.8 49.5 reduce-scatter.2
  178.7 45.8 reduce-scatter.4
Sparse Core Ops, SparseCore 1:
  18.7 128.4 all-gather.2

commit v5 on v4

--- a/solution.py
+++ b/solution.py
@@ -37,15 +37,15 @@
     )
     cycle_part = cycle.reshape(i_win, a_win, jb_dev)
     cycle = lax.psum_scatter(cycle_part, "opair", scatter_dimension=0, tiled=True)
-    cycle = lax.all_to_all(cycle, "vpair", split_axis=1, concat_axis=2, tiled=True)
     v_flat = ladder_ints.reshape(slab_depth, A_DEV * NV)
-    piece = lax.all_gather(
-        amps_rows, "vpair", axis=0, tiled=True
+    piece = lax.all_gather(amps_rows, "vpair", axis=0, tiled=False)
+    ladder = lax.dot_general(
+        piece, v_flat, (((2,), (0,)), ((), ())), preferred_element_type=jnp.float32
     )
-    ladder = jnp.dot(piece, v_flat, preferred_element_type=jnp.float32)
-    ladder = ladder.reshape(i_win, NO, A_DEV * NV)
     ladder, cycle = lax.optimization_barrier((ladder, cycle))
     ladder = lax.psum_scatter(ladder, "opair", scatter_dimension=0, tiled=True)
+    cycle = lax.all_to_all(cycle, "vpair", split_axis=1, concat_axis=2, tiled=True)
+    ladder = ladder.reshape(I_DEV, NO, A_DEV * NV)
     resid = ladder.reshape(I_DEV, NO, A_DEV, NV).transpose(0, 2, 1, 3) + cycle.reshape(
         I_DEV, A_DEV, NO, NV
     )

time: 236 us -> 203 us (0.86)
  blocking collectives: 41.5 us -> 0 us
  waiting for transfers between devices: 125 us -> 142 us
  local copies, waits for them, and re-layouts: 25.4 us -> 11.5 us
  starting transfers between devices: 0.09 us -> 5.44 us
    all_gather x1, waiting for transfers between devices: 36.6 us -> 109 us  [shards(): piece = lax.all_gather(amps_rows, 'vpair', axis=0, tiled=False)]
    reduce_scatter x1, waiting for transfers between devices: 49.1 us -> 0.03 us  [shards(): lax.psum_scatter(cycle_part, 'opair', scatter_dimension=0, tiled=True)]
    all_to_all x1 -> x0, blocking collectives: 41.5 us -> none  [shards(): lax.all_to_all(cycle, 'vpair', split_axis=1, concat_axis=2, tiled=True)]
    reduce_scatter x1, waiting for transfers between devices: 38.9 us -> 14.1 us  [shards(): ladder = lax.psum_scatter(ladder, 'opair', scatter_dimension=0, tiled=True)]
    all_to_all x0 -> x1, waiting for transfers between devices: none -> 18.8 us  [shards(): lax.all_to_all(cycle, 'vpair', split_axis=1, concat_axis=2, tiled=True)]
    dot_general x1 -> x0, local copies, waits for them, and re-layouts: 14.4 us -> none  [shards(): ladder = jnp.dot(piece, v_flat, preferred_element_type=jnp.float32)]
    all_to_all x0 -> x1, starting transfers between devices: none -> 5.35 us  [shards(): lax.all_to_all(cycle, 'vpair', split_axis=1, concat_axis=2, tiled=True)]
  transfers between devices with their start and end apart: 3 -> 4, of which waited for: 3 -> 3; matrix products, arithmetic and copies ran while one was open for 3% -> 15% of each run, Pallas kernels for 0% -> 0%
where the time goes in v5:
time: 203 us
  waiting for transfers between devices  142 us (70%)
  matrix products  23.1 us (11%)
  between operations  16.3 us (8%)
  local copies, waits for them, and re-layouts  11.5 us (6%)
  starting transfers between devices  5.44 us (3%)
  other arithmetic  4.35 us (2%)
    all_gather x1, waiting for transfers between devices, shards(): piece = lax.all_gather(amps_rows, 'vpair', axis=0, tiled=False)  109 us
    all_to_all x1, waiting for transfers between devices, shards(): lax.all_to_all(cycle, 'vpair', split_axis=1, concat_axis=2, tiled=True)  18.8 us
    dot_general x1, matrix products, shards(): lax.dot_general(piece, v_flat, (((2,), (0,)), ((), ())), preferred_elemen...  17.5 us
    reduce_scatter x1, waiting for transfers between devices, shards(): ladder = lax.psum_scatter(ladder, 'opair', scatter_dimension=0, tiled=True)  14.1 us
    dot_general x1, matrix products, shards(): lax.dot_general(cycle_amps, cycle_ints, (((0, 1), (0, 1)), ((), ())), pre...  5.6 us
    all_to_all x1, starting transfers between devices, shards(): lax.all_to_all(cycle, 'vpair', split_axis=1, concat_axis=2, tiled=True)  5.35 us
  transfers between devices with their start and end apart: 4, of which 3 were waited for; matrix products, arithmetic and copies ran while one was open for 15% of the time, Pallas kernels for 0%

profile of v5, /device:TPU:1, one launch (start us, length us, event | category | flops | bytes accessed | tf_op | source)
XLA Modules:
  0.0 202.8 jit_solution(1044180460733060446)
XLA Ops:
  7.4 0.0 copy-start
  7.4 0.0 all-gather.4.cloned.1.call-start
  7.4 1.4 copy.25
  8.8 1.2 reshape.183
  10.0 0.0 all-gather.4.cloned.1.call-update
  10.0 0.0 reduce-scatter.3.cloned.1.call-start
  10.1 0.0 copy-done
  10.1 5.6 %fusion.3 = f32[512,3125,1]{1,0,2:T(8,128)} fusion(bf16[3,100,512]{2,1,0:T(8,128)(2,1)} %param.12, bf16[3,100,3125]{2,1,0:T(8,128)(2,1)S(1)} %copy-done), kind=kOutput, calls=%fused_computation.18 | convolution fusion | flops 960000000 | bytes 8582200 | tf_op jit(solution)/shard_map/dot_general | solution.py:35
  15.7 0.0 reduce-scatter.3.cloned.1.call-update
  15.7 0.0 reduce-scatter.5.cloned.1.call-start
  15.8 109.1 %all-gather.4.cloned.1.call-done = bf16[32,50,3000]{2,1,0:T(8,128)(2,1)} async-done(((bf16[1,50,3000]{2,1,0:T(8,128)(2,1)}), bf16[32,50,3000]{2,1,0:T(8,128)(2,1)}) %all-gather.4.cloned.1.call-update) | async-done | bytes 9600016 | tf_op jit(solution)/shard_map/all_gather | solution.py:41
  124.9 17.5 %fusion.2 = f32[32,50,1000]{2,1,0:T(8,128)} fusion(bf16[32,50,3000]{2,1,0:T(8,128)(2,1)} %all-gather.4.cloned.1.call-done, bf16[3000,1000,1]{1,0,2:T(8,128)(2,1)} %bitcast.24), kind=kOutput, calls=%fused_computation.17 | convolution fusion | flops 9600000000 | bytes 22000000 | tf_op jit(solution)/shard_map/dot_general | solution.py:42
  142.4 0.0 copy-start.4
  142.4 0.0 copy-start.5
  142.4 0.0 copy-start.2
  142.4 0.0 copy-start.3
  142.5 0.0 reduce-scatter.3.cloned.1.call-done
  142.5 0.0 copy-start.1
  142.5 0.0 reduce-scatter.5.cloned.1.call-update
  143.9 0.0 copy-done.4
  143.9 0.2 reduce-window.9
  144.1 0.0 copy-done.5
  144.1 0.2 reduce-window.6
  144.3 0.0 copy-done.2
  144.3 0.7 dynamic_slice.7
  144.9 0.0 copy-done.1
  144.9 1.5 copy.27
  146.5 5.3 %all-to-all-start = ((f32[2,32,3125]{2,0,1:T(2,128)}), f32[2,32,3125]{2,0,1:T(2,128)S(1)}, u32[]{:S(2)}, u32[]{:S(2)}) async-start(f32[2,32,3125]{2,0,1:T(2,128)} %copy.27), calls=%async_computation.2 | async-start | bytes 1638400 | tf_op jit(solution)/shard_map/all_to_all | solution.py:47
  151.8 0.0 copy-done.3
  151.8 0.7 dynamic-slice_subtract_fusion
  152.5 0.7 fusion.1
  153.2 0.1 convert_reduce_fusion
  153.3 0.1 convert_reduce_fusion.1
  153.4 0.2 fusion
  153.6 0.6 broadcast_xor_fusion.1
  154.2 0.1 broadcast_add_fusion
  154.3 0.1 broadcast_xor_fusion
  154.4 18.8 %all-to-all-done = f32[2,32,3125]{2,0,1:T(2,128)S(1)} async-done(((f32[2,32,3125]{2,0,1:T(2,128)}), f32[2,32,3125]{2,0,1:T(2,128)S(1)}, u32[]{:S(2)}, u32[]{:S(2)}) %all-to-all-start) | async-done | bytes 800032 | tf_op jit(solution)/shard_map/all_to_all | solution.py:47
  173.1 0.9 copy.28
  174.1 1.7 reshape.186
  175.8 14.1 %reduce-scatter.5.cloned.1.call-done = f32[4,50,1000]{2,1,0:T(8,128)} async-done(((f32[32,50,1000]{2,1,0:T(8,128)}), f32[4,50,1000]{2,1,0:T(8,128)}) %reduce-scatter.5.cloned.1.call-update) | async-done | bytes 800016 | tf_op jit(solution)/shard_map/reduce_scatter | solution.py:46
  189.9 2.2 %transpose_reshape_reshape.3 = f32[2,1,100,1000]{3,2,0,1:T(8,128)} reshape(f32[4,50,1000]{2,1,0:T(8,128)} %reduce-scatter.5.cloned.1.call-done) | data formatting | bytes 1600000 | tf_op jit(solution)/shard_map/transpose;reshape;reshape | solution.py:49
  192.1 1.5 divide_select_fusion
  193.6 1.7 copy.29
  (2 shorter events, 0.0 us)
Async XLA Ops:
  7.4 2.7 %copy-start = (bf16[3,100,3125]{2,1,0:T(8,128)(2,1)S(1)}, bf16[3,100,3125]{2,1,0:T(8,128)(2,1)}, u32[]{:S(2)}) copy-start(bf16[3,100,3125]{2,1,0:T(8,128)(2,1)} %param.13) | copy-start | bytes 5625004
  7.4 117.5 %all-gather.4.cloned.1.call-start = ((), (), s32[]{:S(2)}) async-start(), calls=%async_computation.5 | async-start | bytes 11354112 | tf_op jit(solution)/shard_map/all_gather | solution.py:41
  10.0 132.4 %reduce-scatter.3.cloned.1.call-start = ((), (), s32[]{:S(2)}) async-start(), calls=%async_computation.3 | async-start | bytes 7372800 | tf_op jit(solution)/shard_map/reduce_scatter | solution.py:39
  15.7 174.2 %reduce-scatter.5.cloned.1.call-start = ((), (), s32[]{:S(2)}) async-start(), calls=%async_computation.4 | async-start | bytes 8257536 | tf_op jit(solution)/shard_map/reduce_scatter | solution.py:46
  142.4 1.5 copy-start.4
  142.4 1.7 copy-start.5
  142.4 1.8 copy-start.2
  142.4 9.4 %copy-start.3 = (f32[100]{0:T(128)S(1)}, f32[100]{0:T(128)}, u32[]{:S(2)}) copy-start(f32[100]{0:T(128)} %param.18) | copy-start | bytes 1204
  142.5 2.4 %copy-start.1 = (f32[2,32,3125]{2,1,0:T(8,128)S(1)}, f32[2,32,3125]{2,1,0:T(8,128)}, u32[]{:S(2)}) copy-start(f32[2,32,3125]{2,1,0:T(8,128)} %reduce-scatter.3.cloned.1.call-done) | copy-start | bytes 2400004
  146.5 26.7 %all-to-all-start = ((f32[2,32,3125]{2,0,1:T(2,128)}), f32[2,32,3125]{2,0,1:T(2,128)S(1)}, u32[]{:S(2)}, u32[]{:S(2)}) async-start(f32[2,32,3125]{2,0,1:T(2,128)} %copy.27), calls=%async_computation.2 | async-start | bytes 1638400 | tf_op jit(solution)/shard_map/all_to_all | solution.py:47
Sparse Core Ops, SparseCore 0:
  10.7 114.1 all-gather.3
Sparse Core Ops, SparseCore 1:
  15.8 49.5 reduce-scatter.2
  142.6 47.3 reduce-scatter.4

commit v6 on v5

--- a/solution.py
+++ b/solution.py
@@ -45,31 +45,27 @@
     ladder, cycle = lax.optimization_barrier((ladder, cycle))
     ladder = lax.psum_scatter(ladder, "opair", scatter_dimension=0, tiled=True)
     cycle = lax.all_to_all(cycle, "vpair", split_axis=1, concat_axis=2, tiled=True)
-    ladder = ladder.reshape(I_DEV, NO, A_DEV * NV)
-    resid = ladder.reshape(I_DEV, NO, A_DEV, NV).transpose(0, 2, 1, 3) + cycle.reshape(
-        I_DEV, A_DEV, NO, NV
-    )
+    n_blk, n_row = ladder.shape[0], ladder.shape[1]
+    resid = ladder + cycle.reshape(n_blk, n_row, NV)
     first_occ = occ_start[0] + lax.axis_index("opair") * I_DEV
     first_virt = virt_start[0] + lax.axis_index("vpair") * A_DEV
     glob_i = first_occ + jnp.arange(I_DEV, dtype=jnp.int32)
     glob_a = first_virt + jnp.arange(A_DEV, dtype=jnp.int32)
-    sym_i = irrep_of(occ_blocks, glob_i)
+    per_i = n_blk // I_DEV
+    sym_i = jnp.repeat(irrep_of(occ_blocks, glob_i), per_i)
     sym_a = irrep_of(virt_blocks, glob_a)
-    sym_j = irrep_of(occ_blocks, jnp.arange(NO, dtype=jnp.int32))
+    sym_j = jnp.tile(irrep_of(occ_blocks, jnp.arange(NO, dtype=jnp.int32)).reshape(per_i, n_row), (I_DEV, 1))
     sym_b = irrep_of(virt_blocks, jnp.arange(NV, dtype=jnp.int32))
     total_sym = jnp.bitwise_xor(
-        jnp.bitwise_xor(sym_i[:, None, None, None], sym_a[None, :, None, None]),
-        jnp.bitwise_xor(sym_j[None, None, :, None], sym_b[None, None, None, :]),
+        jnp.bitwise_xor(sym_i[:, None, None], sym_a[0]),
+        jnp.bitwise_xor(sym_j[:, :, None], sym_b[None, None, :]),
     )
-    e_i = lax.dynamic_slice_in_dim(eps_occ, first_occ, I_DEV)
+    e_i = jnp.repeat(lax.dynamic_slice_in_dim(eps_occ, first_occ, I_DEV), per_i)
     e_a = lax.dynamic_slice_in_dim(eps_virt, first_virt, A_DEV)
-    denom = (
-        e_i[:, None, None, None]
-        - e_a[None, :, None, None]
-        + eps_occ[None, None, :, None]
-        - eps_virt[None, None, None, :]
-    )
-    return jnp.where(total_sym == 0, resid / denom, jnp.float32(0.0))
+    e_j = jnp.tile(eps_occ.reshape(per_i, n_row), (I_DEV, 1))
+    denom = e_i[:, None, None] - e_a[0] + e_j[:, :, None] - eps_virt[None, None, :]
+    update = jnp.where(total_sym == 0, resid / denom, jnp.float32(0.0))
+    return update.reshape(I_DEV, A_DEV, NO, NV)
 
 
 def solution(mesh):

time: 203 us -> 203 us (level)
    reshape x1 -> x2, local copies, waits for them, and re-layouts: 1.73 us -> 5.13 us  [the longest x1 3.1 us: shards(): return update.reshape(I_DEV, A_DEV, NO, NV)]
    all_to_all x1, waiting for transfers between devices: 18.8 us -> 16.1 us  [shards(): lax.all_to_all(cycle, 'vpair', split_axis=1, concat_axis=2, tiled=True)]
    another operation x1 -> x4, local copies, waits for them, and re-layouts: 2.2 us -> 0.17 us  [the longest x2 0.09 us: shards(): jnp.tile(irrep_of(occ_blocks, jnp.arange(NO, dtype=jnp.int32)).reshape(pe...]
where the time goes in v6:
time: 203 us
  waiting for transfers between devices  140 us (69%)
  matrix products  23.1 us (11%)
  between operations  16.3 us (8%)
  local copies, waits for them, and re-layouts  12.5 us (6%)
  starting transfers between devices  5.44 us (3%)
  other arithmetic  5.22 us (3%)
    all_gather x1, waiting for transfers between devices, shards(): piece = lax.all_gather(amps_rows, 'vpair', axis=0, tiled=False)  109 us
    dot_general x1, matrix products, shards(): lax.dot_general(piece, v_flat, (((2,), (0,)), ((), ())), preferred_elemen...  17.5 us
    all_to_all x1, waiting for transfers between devices, shards(): lax.all_to_all(cycle, 'vpair', split_axis=1, concat_axis=2, tiled=True)  16.1 us
    reduce_scatter x1, waiting for transfers between devices, shards(): ladder = lax.psum_scatter(ladder, 'opair', scatter_dimension=0, tiled=True)  15.1 us
    dot_general x1, matrix products, shards(): lax.dot_general(cycle_amps, cycle_ints, (((0, 1), (0, 1)), ((), ())), pre...  5.6 us
    all_to_all x1, starting transfers between devices, shards(): lax.all_to_all(cycle, 'vpair', split_axis=1, concat_axis=2, tiled=True)  5.35 us
  transfers between devices with their start and end apart: 4, of which 3 were waited for; matrix products, arithmetic and copies ran while one was open for 15% of the time, Pallas kernels for 0%

profile of v6, /device:TPU:1, one launch (start us, length us, event | category | flops | bytes accessed | tf_op | source)
XLA Modules:
  0.0 203.0 jit_solution(13357941858486845523)
XLA Ops:
  7.4 0.0 copy-start
  7.4 0.0 all-gather.4.cloned.1.call-start
  7.4 1.4 copy.22
  8.8 1.2 reshape.118
  10.0 0.0 all-gather.4.cloned.1.call-update
  10.0 0.0 reduce-scatter.3.cloned.1.call-start
  10.1 0.0 copy-done
  10.1 5.6 %fusion.3 = f32[512,3125,1]{1,0,2:T(8,128)} fusion(bf16[3,100,512]{2,1,0:T(8,128)(2,1)} %param.12, bf16[3,100,3125]{2,1,0:T(8,128)(2,1)S(1)} %copy-done), kind=kOutput, calls=%fused_computation.17 | convolution fusion | flops 960000000 | bytes 8582200 | tf_op jit(solution)/shard_map/dot_general | solution.py:35
  15.7 0.0 reduce-scatter.3.cloned.1.call-update
  15.7 0.0 reduce-scatter.5.cloned.1.call-start
  15.8 109.1 %all-gather.4.cloned.1.call-done = bf16[32,50,3000]{2,1,0:T(8,128)(2,1)} async-done(((bf16[1,50,3000]{2,1,0:T(8,128)(2,1)}), bf16[32,50,3000]{2,1,0:T(8,128)(2,1)}) %all-gather.4.cloned.1.call-update) | async-done | bytes 9600016 | tf_op jit(solution)/shard_map/all_gather | solution.py:41
  124.9 17.5 %fusion.2 = f32[32,50,1000]{2,1,0:T(8,128)} fusion(bf16[32,50,3000]{2,1,0:T(8,128)(2,1)} %all-gather.4.cloned.1.call-done, bf16[3000,1000,1]{1,0,2:T(8,128)(2,1)} %bitcast.28), kind=kOutput, calls=%fused_computation.16 | convolution fusion | flops 9600000000 | bytes 22000000 | tf_op jit(solution)/shard_map/dot_general | solution.py:42
  142.4 0.0 copy-start.3
  142.4 0.0 copy-start.2
  142.4 0.0 copy-start.4
  142.4 0.0 copy-start.5
  142.5 0.0 reduce-scatter.3.cloned.1.call-done
  142.5 0.0 copy-start.1
  142.5 0.0 reduce-scatter.5.cloned.1.call-update
  142.5 1.1 copy-done.1
  143.6 1.5 copy.24
  145.2 5.3 %all-to-all-start = ((f32[2,32,3125]{2,0,1:T(2,128)}), f32[2,32,3125]{2,0,1:T(2,128)S(1)}, u32[]{:S(2)}, u32[]{:S(2)}) async-start(f32[2,32,3125]{2,0,1:T(2,128)} %copy.24), calls=%async_computation.2 | async-start | bytes 1638400 | tf_op jit(solution)/shard_map/all_to_all | solution.py:47
  150.5 0.0 copy-done.3
  150.5 0.1 tile.21
  151.9 0.0 copy-done.2
  152.0 0.6 dynamic_slice.7
  152.6 0.7 dynamic-slice_subtract_fusion
  153.3 0.1 broadcast_in_dim.8
  153.3 0.1 sub.30
  153.4 0.0 copy-done.4
  153.4 0.2 reduce-window.9
  153.6 0.0 copy-done.5
  153.6 0.2 reduce-window.6
  153.8 0.1 convert_reduce_fusion.1
  153.9 0.1 tile.18
  154.0 0.7 fusion.1
  154.6 0.2 fusion
  154.8 0.6 broadcast_xor_fusion
  155.4 0.1 broadcast_in_dim.7
  155.5 0.1 xor.38
  155.6 0.1 convert_reduce_fusion
  155.7 0.1 broadcast_add_fusion
  155.7 16.1 %all-to-all-done = f32[2,32,3125]{2,0,1:T(2,128)S(1)} async-done(((f32[2,32,3125]{2,0,1:T(2,128)}), f32[2,32,3125]{2,0,1:T(2,128)S(1)}, u32[]{:S(2)}, u32[]{:S(2)}) %all-to-all-start) | async-done | bytes 800032 | tf_op jit(solution)/shard_map/all_to_all | solution.py:47
  171.8 0.9 copy.25
  172.8 2.0 reshape.121
  174.8 15.1 %reduce-scatter.5.cloned.1.call-done = f32[4,50,1000]{2,1,0:T(8,128)} async-done(((f32[32,50,1000]{2,1,0:T(8,128)}), f32[4,50,1000]{2,1,0:T(8,128)}) %reduce-scatter.5.cloned.1.call-update) | async-done | bytes 800016 | tf_op jit(solution)/shard_map/reduce_scatter | solution.py:46
  189.9 2.5 %divide_select_fusion = f32[4,50,1000]{2,1,0:T(8,128)} fusion(f32[4,50,1000]{2,1,0:T(8,128)} %reduce-scatter.5.cloned.1.call-done, f32[4,50,1000]{2,1,0:T(8,128)S(1)} %reshape.121, f32[1000]{0:T(1024)S(1)} %copy-done.2, f32[4,50]{1,0:T(4,128)S(1)} %broadcast_add_fusion, s32[1000]{0:T(1024)S(1)} %convert_reduce_fusion, s32[4,50]{1,0:T(4,128)S(1)} %bitcast.26, ...), kind=kLoop, calls=%fused_computation | loop fusion | flops 1400000 | bytes 2409616 | tf_op jit(solution)/shard_map/jit(_where)/select_n | solution.py:67
  192.4 3.1 %reshape.129 = f32[2,1,100,1000]{3,1,2,0:T(1,128)} reshape(f32[4,50,1000]{2,1,0:T(8,128)} %divide_select_fusion) | data formatting | bytes 1600000 | tf_op jit(solution)/shard_map/reshape | solution.py:68
  (4 shorter events, 0.0 us)
Async XLA Ops:
  7.4 2.7 %copy-start = (bf16[3,100,3125]{2,1,0:T(8,128)(2,1)S(1)}, bf16[3,100,3125]{2,1,0:T(8,128)(2,1)}, u32[]{:S(2)}) copy-start(bf16[3,100,3125]{2,1,0:T(8,128)(2,1)} %param.13) | copy-start | bytes 5625004
  7.4 117.5 %all-gather.4.cloned.1.call-start = ((), (), s32[]{:S(2)}) async-start(), calls=%async_computation.5 | async-start | bytes 11354112 | tf_op jit(solution)/shard_map/all_gather | solution.py:41
  10.0 132.4 %reduce-scatter.3.cloned.1.call-start = ((), (), s32[]{:S(2)}) async-start(), calls=%async_computation.3 | async-start | bytes 7372800 | tf_op jit(solution)/shard_map/reduce_scatter | solution.py:39
  15.7 174.2 %reduce-scatter.5.cloned.1.call-start = ((), (), s32[]{:S(2)}) async-start(), calls=%async_computation.4 | async-start | bytes 8257536 | tf_op jit(solution)/shard_map/reduce_scatter | solution.py:46
  142.4 8.1 %copy-start.3 = (f32[100]{0:T(128)S(1)}, f32[100]{0:T(128)}, u32[]{:S(2)}) copy-start(f32[100]{0:T(128)} %param.18) | copy-start | bytes 1204
  142.4 9.5 %copy-start.2 = (f32[1000]{0:T(1024)S(1)}, f32[1000]{0:T(1024)}, u32[]{:S(2)}) copy-start(f32[1000]{0:T(1024)} %param.19) | copy-start | bytes 12004
  142.4 11.0 %copy-start.4 = (s32[8]{0:T(128)S(1)}, s32[8]{0:T(128)}, u32[]{:S(2)}) copy-start(s32[8]{0:T(128)} %param.15) | copy-start | bytes 100
  142.4 11.2 %copy-start.5 = (s32[8]{0:T(128)S(1)}, s32[8]{0:T(128)}, u32[]{:S(2)}) copy-start(s32[8]{0:T(128)} %param.14) | copy-start | bytes 100
  142.5 1.2 copy-start.1
  145.2 26.7 %all-to-all-start = ((f32[2,32,3125]{2,0,1:T(2,128)}), f32[2,32,3125]{2,0,1:T(2,128)S(1)}, u32[]{:S(2)}, u32[]{:S(2)}) async-start(f32[2,32,3125]{2,0,1:T(2,128)} %copy.24), calls=%async_computation.2 | async-start | bytes 1638400 | tf_op jit(solution)/shard_map/all_to_all | solution.py:47
Sparse Core Ops, SparseCore 0:
  10.7 114.1 all-gather.3
Sparse Core Ops, SparseCore 1:
  15.8 49.5 reduce-scatter.2
  142.6 47.3 reduce-scatter.4
